TPU v7x, 512 devices: a whole 4x4x16 slice. The times are simulated.
512 devices in a mesh: section: 4 (over x), expert: 16 (over z), rep: 8 (over y, core).
Axes of the slice: x: 4, y: 4, z: 16, core: 2. Of those that a mesh axis runs over, the one named last changes fastest.
Arguments:
- tokens: bfloat16 [4, 2048, 4096], P('section', 'expert', 'rep'), may hold values from -6 to 6
- expert_ids: int32 [4, 2048, 2], P('section', 'expert'), may hold values from 0 to 15, all different within a row; in each aligned block of 128 rows (0 to 127, 128 to 255, ..., all dimensions but the last counted through in order) at most 20 rows name the same one
- route_weight: float32 [4, 2048, 2], P('section', 'expert'), may hold values from 0.05 to 0.5
- language: int32 [4, 2048], P('section', 'expert'), may hold values from 0 to 3
- capacity: int32 [4, 16], replicated, may hold values from 0 to 7
- spill_table: int32 [4, 16], P('section'), may hold values from 0 to 15, as said below
- w_gate: bfloat16 [4, 16, 4096, 1024], P('section', 'expert', None, 'rep'), may hold values from -0.09375 to 0.09375
- w_up: bfloat16 [4, 16, 4096, 1024], P('section', 'expert', None, 'rep'), may hold values from -0.09375 to 0.09375
- w_down: bfloat16 [4, 16, 1024, 4096], P('section', 'expert', None, 'rep'), may hold values from -0.1875 to 0.1875
Outputs:
- next_rows: bfloat16 [4, 2048, 4096], P('section', 'expert', 'rep')
Inputs may be any that keep to these rules, and one draw needn't show every extreme that they name: `expert_ids`: each token names 2 different experts. Among the tokens of one index of expert (aligned blocks of 128 rows, sections in order) no expert is named by more than 20 tokens, a bound that some block reaches. `spill_table`: in each section's row every expert names another expert, and every expert is named by exactly one; each row is one cycle through all 16.
All inputs are finite; a program needn't handle non-finite values.
Results may differ from a plain program's by a relative error of at most 0.0057.
Values may be sent and summed in bfloat16 or wider, within the bound.
No kernel may reach another device: no remote copies, remote signals or barrier semaphores. Data moves between devices by JAX's collectives and lax.ppermute only.
A program may use at most 64 MiB of HBM per device.

v0:
```python
import jax
import jax.numpy as jnp
from jax import lax
from jax.sharding import PartitionSpec as P


def passed_along(value, axis, steps):
    count = lax.axis_size(axis)
    pairs = [(source, (source + steps) % count) for source in range(count)]
    return lax.ppermute(value, axis, pairs)


def admission(chosen, language, capacity, experts):
    lang_count = capacity.shape[0]
    hit_table = jnp.sum(
        (chosen[:, :, None] == jnp.arange(experts, dtype=jnp.int32)[None, None, :]).astype(
            jnp.int32
        ),
        axis=1,
    )
    lang_hot = (language[:, None] == jnp.arange(lang_count, dtype=jnp.int32)[None, :]).astype(
        jnp.int32
    )
    lang_hits = lang_hot[:, :, None] * hit_table[:, None, :]
    before = jnp.cumsum(lang_hits, axis=0) - lang_hits
    place_rank = jnp.sum(before * lang_hot[:, :, None], axis=1)
    allowance = jnp.sum(lang_hot[:, :, None] * capacity[None, :, :], axis=1)
    admitted = hit_table * (place_rank < allowance).astype(jnp.int32)
    return (hit_table, admitted)


def slot_sources(markers, slot_table, slot_depth):
    tok_rows = markers.shape[0]
    selected = markers[:, :, None] * (
        slot_table[:, :, None] == jnp.arange(slot_depth, dtype=jnp.int32)[None, None, :]
    ).astype(jnp.int32)
    positions = jnp.arange(tok_rows, dtype=jnp.int32)[:, None, None]
    source = jnp.sum(selected * positions, axis=0)
    filled = jnp.sum(selected, axis=0)
    return jnp.where(filled > 0, source, tok_rows)


def local(tokens, expert_ids, route_weight, language, capacity, spill_table, w_gate, w_up, w_down):
    experts = lax.axis_size("expert")
    chosen = expert_ids[0]
    spill_row = spill_table[0]
    tok_rows, top_count = chosen.shape
    slot_depth = min(tok_rows, max(2, 5 * tok_rows * top_count // (4 * experts)))
    expert_iota = jnp.arange(experts, dtype=jnp.int32)
    hit_table, admitted = admission(chosen, language[0], capacity, experts)
    spilled = hit_table - admitted
    main_slot = jnp.cumsum(admitted, axis=0) - admitted
    spill_slot = jnp.cumsum(spilled, axis=0) - spilled
    spill_move = (spill_row[:, None] == expert_iota[None, :]).astype(jnp.int32)
    spill_marks = jnp.sum(spilled[:, :, None] * spill_move[None, :, :], axis=1)
    spill_places = jnp.sum((spill_slot * spilled)[:, :, None] * spill_move[None, :, :], axis=1)
    row_source = lax.all_gather(tokens[0], "rep", axis=1, tiled=True)
    with_blank = jnp.concatenate(
        [row_source, jnp.zeros((1, row_source.shape[1]), row_source.dtype)], axis=0
    )
    main_source = slot_sources(admitted, main_slot, slot_depth)
    spill_source = slot_sources(spill_marks, spill_places, slot_depth)
    outgoing = jnp.take(with_blank, jnp.stack([main_source, spill_source]), axis=0)
    arrived = jnp.stack(
        [
            lax.all_to_all(outgoing[0], "expert", split_axis=0, concat_axis=0, tiled=True),
            lax.all_to_all(outgoing[1], "expert", split_axis=0, concat_axis=0, tiled=True),
        ]
    )
    feat_width = arrived.shape[3]
    flattened = arrived.reshape(-1, feat_width)
    gate_proj = jnp.dot(flattened, w_gate[0, 0], preferred_element_type=jnp.float32)
    up_proj = jnp.dot(flattened, w_up[0, 0], preferred_element_type=jnp.float32)
    activated = (jax.nn.silu(gate_proj) * up_proj).astype(jnp.bfloat16)
    down_local = w_down[0, 0]
    produced = jnp.dot(
        lax.all_gather(activated, "rep", axis=1, tiled=True),
        down_local,
        preferred_element_type=jnp.float32,
    )
    produced = produced.astype(jnp.bfloat16).reshape(2, experts, slot_depth, down_local.shape[1])
    returned = jnp.stack(
        [
            lax.all_to_all(produced[0], "expert", split_axis=0, concat_axis=0, tiled=True),
            lax.all_to_all(produced[1], "expert", split_axis=0, concat_axis=0, tiled=True),
        ]
    )
    id_match = (chosen[:, :, None] == expert_iota[None, None, :]).astype(jnp.int32)
    row_kept = jnp.sum(id_match * admitted[:, None, :], axis=2)
    row_main = jnp.sum(id_match * main_slot[:, None, :], axis=2)
    row_spill = jnp.sum(id_match * spill_slot[:, None, :], axis=2)
    row_other = jnp.sum(id_match * spill_row[None, None, :], axis=2)
    target = jnp.where(row_kept > 0, chosen, row_other)
    slot_pick = jnp.where(row_kept > 0, row_main, row_spill)
    row_index = (1 - row_kept) * experts * slot_depth + target * slot_depth + slot_pick
    out_width = returned.shape[3]
    picked = jnp.take(returned.reshape(-1, out_width), row_index.reshape(-1), axis=0).reshape(
        tok_rows, top_count, out_width
    )
    combined = jnp.sum(route_weight[0][:, :, None] * picked.astype(jnp.float32), axis=1).astype(
        jnp.bfloat16
    )
    forwarded = passed_along(combined, "section", 1)
    return forwarded[None]


def solution(mesh):
    in_specs = (
        P("section", "expert", "rep"),
        P("section", "expert", None),
        P("section", "expert", None),
        P("section", "expert"),
        P(),
        P("section", None),
        P("section", "expert", None, "rep"),
        P("section", "expert", None, "rep"),
        P("section", "expert", None, "rep"),
    )
    out_specs = P("section", "expert", "rep")
    return jax.shard_map(local, mesh=mesh, in_specs=in_specs, out_specs=out_specs, check_vma=False)
```

profile of v0, /device:TPU:16, one launch (start us, length us, event | category | flops | bytes accessed | tf_op | source)
XLA Modules:
  0.0 496.3 jit_solution(13053874309466298952)
XLA Ops:
  6.5 0.7 all-gather.6.cloned.1.call-update
  7.3 0.7 convert_reduce_fusion
  8.1 0.7 fusion.13
  8.8 1.2 multiply_reduce_fusion.1
  10.1 0.2 reduce_window_sum.30
  10.3 0.2 reduce_window_sum.29
  10.7 0.7 fusion.14
  11.5 0.7 select_reduce_fusion
  12.3 0.8 select_reduce_fusion.1
  13.4 30.4 %all-gather.6.cloned.1.call-done = bf16[1,128,4096]{2,1,0:T(8,128)(2,1)} async-done(((bf16[1,128,512]{2,1,0:T(8,128)(2,1)}), bf16[1,128,4096]{2,1,0:T(8,128)(2,1)}) %all-gather.6.cloned.1.call-update) | async-done | bytes 1048592 | tf_op jit(solution)/shard_map/all_gather | solution.py:57
  43.8 1.3 concatenate.24
  45.1 5.4 %gather_fusion = bf16[640,4096]{1,0:T(8,128)(2,1)} fusion(bf16[129,4096]{1,0:T(8,128)(2,1)S(1)} %concatenate.24, s32[1024]{0:T(1024)S(1)} %pad_clamp_fusion.1), kind=kCustom, calls=%fused_computation | custom fusion | bytes 10488320 | tf_op jit(solution)/shard_map/jit(_take)/gather | solution.py:63
  50.5 7.7 %reshape.378 = bf16[2,16,20,4096]{3,2,1,0:T(8,128)(2,1)} reshape(bf16[640,4096]{1,0:T(8,128)(2,1)} %gather_fusion) | data formatting | bytes 10485760 | tf_op jit(solution)/shard_map/jit(_take)/gather | solution.py:63
  58.2 3.4 broadcast_select_fusion
  61.6 0.7 slice_bitcast_fusion.1
  62.4 153.6 %all_to_all.20 = bf16[16,20,4096]{2,1,0:T(8,128)(2,1)S(1)} all-to-all(bf16[16,20,4096]{2,1,0:T(8,128)(2,1)S(1)} %get-tuple-element.23), channel_id=1, replica_groups=mesh['section'=4,'expert'=16,'rep'=8] {'expert'}, dimensions={0} | all-to-all | bytes 5242880 | tf_op jit(solution)/shard_map/all_to_all | solution.py:66
  215.9 147.8 %all_to_all.21 = bf16[16,20,4096]{2,1,0:T(8,128)(2,1)S(1)} all-to-all(bf16[16,20,4096]{2,1,0:T(8,128)(2,1)S(1)} %get-tuple-element.24), channel_id=1, replica_groups=mesh['section'=4,'expert'=16,'rep'=8] {'expert'}, dimensions={0} | all-to-all | bytes 5242880 | tf_op jit(solution)/shard_map/all_to_all | solution.py:67
  363.7 3.4 pad_maximum_fusion
  367.1 7.9 %reshape.375 = bf16[640,4096]{1,0:T(8,128)(2,1)} reshape(bf16[2,16,20,4096]{3,2,1,0:T(8,128)(2,1)} %pad_maximum_fusion) | data formatting | bytes 10485760 | tf_op jit(solution)/shard_map/reshape | solution.py:71
  375.0 4.1 fusion.3
  379.2 0.2 copy-done.6
  379.3 2.2 fusion
  381.6 27.1 %all-gather.4.cloned.1.call-done = bf16[640,1024]{1,0:T(8,128)(2,1)} async-done(((bf16[640,128]{1,0:T(8,128)(2,1)}), bf16[640,1024]{1,0:T(8,128)(2,1)}) %all-gather.4.cloned.1.call-update) | async-done | bytes 1310736 | tf_op jit(solution)/shard_map/all_gather | solution.py:77
  408.7 2.2 convolution_convert_fusion
  410.9 0.8 squeeze.33
  411.7 12.3 %all-to-all-start.2 = ((bf16[16,20,512]{2,1,0:T(8,128)(2,1)}), bf16[16,20,512]{2,1,0:T(8,128)(2,1)S(1)}, u32[]{:S(2)}, u32[]{:S(2)}) async-start(bf16[16,20,512]{2,1,0:T(8,128)(2,1)} %squeeze.33), calls=%async_computation.2 | async-start | bytes 786432 | tf_op jit(solution)/shard_map/all_to_all | solution.py:84
  424.0 0.8 squeeze.34
  424.8 23.7 %all-to-all-done.2 = bf16[16,20,512]{2,1,0:T(8,128)(2,1)S(1)} async-done(((bf16[16,20,512]{2,1,0:T(8,128)(2,1)}), bf16[16,20,512]{2,1,0:T(8,128)(2,1)S(1)}, u32[]{:S(2)}, u32[]{:S(2)}) %all-to-all-start.2) | async-done | bytes 327712 | tf_op jit(solution)/shard_map/all_to_all | solution.py:84
  448.5 5.7 %all-to-all-start.3 = ((bf16[16,20,512]{2,1,0:T(8,128)(2,1)}), bf16[16,20,512]{2,1,0:T(8,128)(2,1)S(1)}, u32[]{:S(2)}, u32[]{:S(2)}) async-start(bf16[16,20,512]{2,1,0:T(8,128)(2,1)} %squeeze.34), calls=%async_computation.3 | async-start | bytes 786432 | tf_op jit(solution)/shard_map/all_to_all | solution.py:85
  454.2 0.1 copy.57
  454.5 0.1 copy.58
  454.8 0.1 copy.56
  455.0 0.1 gt.67
  455.1 0.1 copy.55
  455.2 0.1 mul.221
  455.4 0.1 reduce_sum.145
  455.5 0.1 reduce_sum.146
  455.7 0.1 reduce_sum.147
  455.8 0.1 squeeze.35
  455.9 0.1 copy.48
  456.1 0.1 copy.41
  456.2 22.1 %all-to-all-done.3 = bf16[16,20,512]{2,1,0:T(8,128)(2,1)S(1)} async-done(((bf16[16,20,512]{2,1,0:T(8,128)(2,1)}), bf16[16,20,512]{2,1,0:T(8,128)(2,1)S(1)}, u32[]{:S(2)}, u32[]{:S(2)}) %all-to-all-start.3) | async-done | bytes 327712 | tf_op jit(solution)/shard_map/all_to_all | solution.py:85
  478.4 0.1 reshape.376
  478.6 1.2 gather_fusion.1
  479.8 0.9 multiply_reduce_fusion
  480.7 3.4 collective-permute-start
  484.1 4.7 collective-permute-done
  488.8 0.7 copy.62
  (43 shorter events, 1.5 us)
Async XLA Ops:
  6.5 402.1 %copy-start = (bf16[1,1,1024,512]{3,2,1,0:T(8,128)(2,1)S(1)}, bf16[1,1,1024,512]{3,2,1,0:T(8,128)(2,1)}, u32[]{:S(2)}) copy-start(bf16[1,1,1024,512]{3,2,1,0:T(8,128)(2,1)} %param.17) | copy-start | bytes 3145732
  6.5 37.3 %all-gather.6.cloned.1.call-start = ((), (), s32[]{:S(2)}) async-start(), calls=%async_computation.5 | async-start | bytes 1179648 | tf_op jit(solution)/shard_map/all_gather | solution.py:57
  7.3 401.4 %all-gather.4.cloned.1.call-start = ((), (), s32[]{:S(2)}) async-start(), calls=%async_computation.4 | async-start | bytes 1474560 | tf_op jit(solution)/shard_map/all_gather | solution.py:77
  367.1 7.9 %copy-start.5 = (bf16[1,1,4096,128]{3,2,1,0:T(8,128)(2,1)S(1)}, bf16[1,1,4096,128]{3,2,1,0:T(8,128)(2,1)}, u32[]{:S(2)}) copy-start(bf16[1,1,4096,128]{3,2,1,0:T(8,128)(2,1)} %param.15) | copy-start | bytes 3145732
  375.0 4.2 copy-start.1
  375.0 4.3 copy-start.6
  381.5 72.6 %copy-start.2 = (s32[1,128,2]{1,2,0:T(2,128)S(1)}, s32[1,128,2]{1,2,0:T(2,128)}, u32[]{:S(2)}) copy-start(s32[1,128,2]{1,2,0:T(2,128)} %param.10) | copy-start | bytes 3076
  381.5 72.8 %copy-start.3 = (s32[1,16]{1,0:T(1,128)S(1)}, s32[1,16]{1,0:T(1,128)}, u32[]{:S(2)}) copy-start(s32[1,16]{1,0:T(1,128)} %param.14) | copy-start | bytes 196
  381.5 74.5 %copy-start.4 = (f32[1,128,2]{1,2,0:T(2,128)S(1)}, f32[1,128,2]{1,2,0:T(2,128)}, u32[]{:S(2)}) copy-start(f32[1,128,2]{1,2,0:T(2,128)} %param.11) | copy-start | bytes 3076
  411.7 36.8 %all-to-all-start.2 = ((bf16[16,20,512]{2,1,0:T(8,128)(2,1)}), bf16[16,20,512]{2,1,0:T(8,128)(2,1)S(1)}, u32[]{:S(2)}, u32[]{:S(2)}) async-start(bf16[16,20,512]{2,1,0:T(8,128)(2,1)} %squeeze.33), calls=%async_computation.2 | async-start | bytes 786432 | tf_op jit(solution)/shard_map/all_to_all | solution.py:84
  448.5 29.9 %all-to-all-start.3 = ((bf16[16,20,512]{2,1,0:T(8,128)(2,1)}), bf16[16,20,512]{2,1,0:T(8,128)(2,1)S(1)}, u32[]{:S(2)}, u32[]{:S(2)}) async-start(bf16[16,20,512]{2,1,0:T(8,128)(2,1)} %squeeze.34), calls=%async_computation.3 | async-start | bytes 786432 | tf_op jit(solution)/shard_map/all_to_all | solution.py:85
  480.7 8.1 %collective-permute-start = (bf16[128,512]{1,0:T(8,128)(2,1)S(1)}, bf16[128,512]{1,0:T(8,128)(2,1)S(1)}, u32[]{:S(2)}, u32[]{:S(2)}) collective-permute-start(bf16[128,512]{1,0:T(8,128)(2,1)S(1)} %multiply_reduce_fusion), channel_id=1, source_target_pairs={{0,128},{128,256},{256,384},{384,0},{1,129},{129,257},{257,385},{3... | collective-permute-start | bytes 393224 | tf_op jit(solution)/shard_map/ppermute | solution.py:10
Sparse Core Ops, SparseCore 0:
  9.5 34.2 all-gather.5
  381.7 26.9 all-gather.3
where the time goes:
time: 497 us; the launch traced here: 496 us
  blocking collectives  301 us (61%)
  waiting for transfers between devices  109 us (22%)
  local copies, waits for them, and re-layouts  29.4 us (6%)
  starting transfers between devices  21.4 us (4%)
  between operations  13.6 us (3%)
  other arithmetic  13.3 us (3%)
  matrix products  8.48 us (2%)
    all_to_all x1, blocking collectives, local(): lax.all_to_all(outgoing[0], 'expert', split_axis=0, concat_axis=0, tiled=...  154 us
    all_to_all x1, blocking collectives, local(): lax.all_to_all(outgoing[1], 'expert', split_axis=0, concat_axis=0, tiled=...  148 us
    all_gather x1, waiting for transfers between devices, local(): row_source = lax.all_gather(tokens[0], 'rep', axis=1, tiled=True)  30.4 us
    all_gather x1, waiting for transfers between devices, local(): lax.all_gather(activated, 'rep', axis=1, tiled=True)  27.1 us
    all_to_all x1, waiting for transfers between devices, local(): lax.all_to_all(produced[0], 'expert', split_axis=0, concat_axis=0, tiled=...  23.7 us
    all_to_all x1, waiting for transfers between devices, local(): lax.all_to_all(produced[1], 'expert', split_axis=0, concat_axis=0, tiled=...  22.1 us
    gather x2, local copies, waits for them, and re-layouts, local(): jnp.take(with_blank, jnp.stack([main_source, spill_source]), axis=0)  13.1 us
    all_to_all x1, starting transfers between devices, local(): lax.all_to_all(produced[0], 'expert', split_axis=0, concat_axis=0, tiled=...  12.3 us
  transfers between devices with their start and end apart: 5, of which 5 were waited for; matrix products, arithmetic and copies ran while one was open for 2% of the time, Pallas kernels for 0%

commit v1 on v0

--- a/solution.py
+++ b/solution.py
@@ -74,7 +74,9 @@
     activated = (jax.nn.silu(gate_proj) * up_proj).astype(jnp.bfloat16)
     down_local = w_down[0, 0]
     produced = jnp.dot(
-        lax.all_gather(activated, "rep", axis=1, tiled=True),
+        jnp.concatenate(
+            lax.all_to_all(jnp.stack([activated] * lax.axis_size("rep")), "rep", 0, 0), axis=1
+        ),
         down_local,
         preferred_element_type=jnp.float32,
     )

time: 497 us -> 483 us (0.972)
  the two profiles are of different devices: /device:TPU:16 before, /device:TPU:64 now
where the time goes in v1:
time: 483 us; the launch traced here: 482 us
  blocking collectives  322 us (67%)
  waiting for transfers between devices  79.1 us (16%)
  local copies, waits for them, and re-layouts  29.6 us (6%)
  starting transfers between devices  18.2 us (4%)
  between operations  13.6 us (3%)
  other arithmetic  13.3 us (3%)
  matrix products  6.52 us (1%)
    all_to_all x1, blocking collectives, local(): lax.all_to_all(outgoing[0], 'expert', split_axis=0, concat_axis=0, tiled=...  153 us
    all_to_all x1, blocking collectives, local(): lax.all_to_all(outgoing[1], 'expert', split_axis=0, concat_axis=0, tiled=...  148 us
    all_gather x1, waiting for transfers between devices, local(): row_source = lax.all_gather(tokens[0], 'rep', axis=1, tiled=True)  31 us
    all_to_all x1, waiting for transfers between devices, local(): lax.all_to_all(produced[0], 'expert', split_axis=0, concat_axis=0, tiled=...  21.9 us
    all_to_all x1, blocking collectives, local(): lax.all_to_all(jnp.stack([activated] * lax.axis_size('rep')), 'rep', 0, 0)  21.6 us
    all_to_all x1, waiting for transfers between devices, local(): lax.all_to_all(produced[1], 'expert', split_axis=0, concat_axis=0, tiled=...  20.9 us
    gather x2, local copies, waits for them, and re-layouts, local(): jnp.take(with_blank, jnp.stack([main_source, spill_source]), axis=0)  13.1 us
  transfers between devices with their start and end apart: 4, of which 4 were waited for; matrix products, arithmetic and copies ran while one was open for 2% of the time, Pallas kernels for 0%

profile of v1, /device:TPU:64, one launch (start us, length us, event | category | flops | bytes accessed | tf_op | source)
XLA Modules:
  0.0 482.2 jit_solution(4756560035342122490)
XLA Ops:
  6.5 0.7 all-gather.3.cloned.1.call-update
  7.3 0.7 convert_reduce_fusion
  8.1 0.7 fusion.13
  8.8 1.2 multiply_reduce_fusion.1
  10.0 0.2 reduce_window_sum.30
  10.2 0.2 reduce_window_sum.29
  10.6 0.7 fusion.14
  11.5 0.7 select_reduce_fusion
  12.2 0.8 select_reduce_fusion.1
  13.4 31.0 %all-gather.3.cloned.1.call-done = bf16[1,128,4096]{2,1,0:T(8,128)(2,1)} async-done(((bf16[1,128,512]{2,1,0:T(8,128)(2,1)}), bf16[1,128,4096]{2,1,0:T(8,128)(2,1)}) %all-gather.3.cloned.1.call-update) | async-done | bytes 1048592 | tf_op jit(solution)/shard_map/all_gather | solution.py:57
  44.3 1.3 concatenate.24
  45.7 5.4 %gather_fusion = bf16[640,4096]{1,0:T(8,128)(2,1)} fusion(bf16[129,4096]{1,0:T(8,128)(2,1)S(1)} %concatenate.24, s32[1024]{0:T(1024)S(1)} %pad_clamp_fusion.1), kind=kCustom, calls=%fused_computation | custom fusion | bytes 10488320 | tf_op jit(solution)/shard_map/jit(_take)/gather | solution.py:63
  51.0 7.7 %reshape.388 = bf16[2,16,20,4096]{3,2,1,0:T(8,128)(2,1)} reshape(bf16[640,4096]{1,0:T(8,128)(2,1)} %gather_fusion) | data formatting | bytes 10485760 | tf_op jit(solution)/shard_map/jit(_take)/gather | solution.py:63
  58.7 3.4 broadcast_select_fusion
  62.1 0.7 slice_bitcast_fusion.1
  62.9 152.5 %all_to_all.25 = bf16[16,20,4096]{2,1,0:T(8,128)(2,1)S(1)} all-to-all(bf16[16,20,4096]{2,1,0:T(8,128)(2,1)S(1)} %get-tuple-element.23), channel_id=1, replica_groups=mesh['section'=4,'expert'=16,'rep'=8] {'expert'}, dimensions={0} | all-to-all | bytes 5242880 | tf_op jit(solution)/shard_map/all_to_all | solution.py:66
  215.4 147.7 %all_to_all.26 = bf16[16,20,4096]{2,1,0:T(8,128)(2,1)S(1)} all-to-all(bf16[16,20,4096]{2,1,0:T(8,128)(2,1)S(1)} %get-tuple-element.24), channel_id=1, replica_groups=mesh['section'=4,'expert'=16,'rep'=8] {'expert'}, dimensions={0} | all-to-all | bytes 5242880 | tf_op jit(solution)/shard_map/all_to_all | solution.py:67
  363.1 3.4 pad_maximum_fusion
  366.5 7.9 %reshape.383 = bf16[640,4096]{1,0:T(8,128)(2,1)} reshape(bf16[2,16,20,4096]{3,2,1,0:T(8,128)(2,1)} %pad_maximum_fusion) | data formatting | bytes 10485760 | tf_op jit(solution)/shard_map/reshape | solution.py:71
  374.4 4.1 fusion.3
  378.6 0.2 copy-done.6
  378.8 1.5 fusion
  380.3 0.2 copy.57
  380.6 21.6 %all_to_all.27 = bf16[8,640,128]{1,2,0:T(8,128)(2,1)S(1)} all-to-all(bf16[8,640,128]{1,2,0:T(8,128)(2,1)S(1)} %stack.47), channel_id=1, replica_groups=mesh['section'=4,'expert'=16,'rep'=8] {'rep'}, dimensions={0} | all-to-all | bytes 2621440 | tf_op jit(solution)/shard_map/all_to_all | solution.py:78
  402.2 0.9 convolution_convert_fusion
  403.1 0.8 squeeze.33
  403.9 8.0 %all-to-all-start.3 = ((bf16[16,20,512]{2,1,0:T(8,128)(2,1)}), bf16[16,20,512]{2,1,0:T(8,128)(2,1)S(1)}, u32[]{:S(2)}, u32[]{:S(2)}) async-start(bf16[16,20,512]{2,1,0:T(8,128)(2,1)} %squeeze.33), calls=%async_computation.3 | async-start | bytes 786432 | tf_op jit(solution)/shard_map/all_to_all | solution.py:86
  411.9 0.8 squeeze.34
  412.7 21.9 %all-to-all-done.3 = bf16[16,20,512]{2,1,0:T(8,128)(2,1)S(1)} async-done(((bf16[16,20,512]{2,1,0:T(8,128)(2,1)}), bf16[16,20,512]{2,1,0:T(8,128)(2,1)S(1)}, u32[]{:S(2)}, u32[]{:S(2)}) %all-to-all-start.3) | async-done | bytes 327712 | tf_op jit(solution)/shard_map/all_to_all | solution.py:86
  434.6 6.7 %all-to-all-start.4 = ((bf16[16,20,512]{2,1,0:T(8,128)(2,1)}), bf16[16,20,512]{2,1,0:T(8,128)(2,1)S(1)}, u32[]{:S(2)}, u32[]{:S(2)}) async-start(bf16[16,20,512]{2,1,0:T(8,128)(2,1)} %squeeze.34), calls=%async_computation.4 | async-start | bytes 786432 | tf_op jit(solution)/shard_map/all_to_all | solution.py:87
  441.4 0.1 copy.60
  441.6 0.1 copy.61
  442.0 0.1 copy.59
  442.1 0.1 gt.67
  442.3 0.1 copy.58
  442.4 0.1 mul.221
  442.5 0.1 reduce_sum.145
  442.7 0.1 reduce_sum.146
  442.8 0.1 reduce_sum.147
  443.0 0.1 squeeze.35
  443.1 0.1 copy.50
  443.4 20.9 %all-to-all-done.4 = bf16[16,20,512]{2,1,0:T(8,128)(2,1)S(1)} async-done(((bf16[16,20,512]{2,1,0:T(8,128)(2,1)}), bf16[16,20,512]{2,1,0:T(8,128)(2,1)S(1)}, u32[]{:S(2)}, u32[]{:S(2)}) %all-to-all-start.4) | async-done | bytes 327712 | tf_op jit(solution)/shard_map/all_to_all | solution.py:87
  464.4 0.1 reshape.386
  464.5 1.2 gather_fusion.1
  465.8 0.9 multiply_reduce_fusion
  466.6 3.4 collective-permute-start
  470.0 4.7 collective-permute-done
  474.7 0.7 copy.65
  (43 shorter events, 1.7 us)
Async XLA Ops:
  6.5 395.6 %copy-start = (bf16[1,1,1024,512]{3,2,1,0:T(8,128)(2,1)S(1)}, bf16[1,1,1024,512]{3,2,1,0:T(8,128)(2,1)}, u32[]{:S(2)}) copy-start(bf16[1,1,1024,512]{3,2,1,0:T(8,128)(2,1)} %param.17) | copy-start | bytes 3145732
  6.5 37.8 %all-gather.3.cloned.1.call-start = ((), (), s32[]{:S(2)}) async-start(), calls=%async_computation.5 | async-start | bytes 1179648 | tf_op jit(solution)/shard_map/all_gather | solution.py:57
  366.5 7.9 %copy-start.5 = (bf16[1,1,4096,128]{3,2,1,0:T(8,128)(2,1)S(1)}, bf16[1,1,4096,128]{3,2,1,0:T(8,128)(2,1)}, u32[]{:S(2)}) copy-start(bf16[1,1,4096,128]{3,2,1,0:T(8,128)(2,1)} %param.15) | copy-start | bytes 3145732
  374.4 4.2 copy-start.1
  374.4 4.3 copy-start.6
  402.2 39.2 %copy-start.2 = (s32[1,128,2]{1,2,0:T(2,128)S(1)}, s32[1,128,2]{1,2,0:T(2,128)}, u32[]{:S(2)}) copy-start(s32[1,128,2]{1,2,0:T(2,128)} %param.10) | copy-start | bytes 3076
  402.2 39.4 %copy-start.3 = (s32[1,16]{1,0:T(1,128)S(1)}, s32[1,16]{1,0:T(1,128)}, u32[]{:S(2)}) copy-start(s32[1,16]{1,0:T(1,128)} %param.14) | copy-start | bytes 196
  402.2 41.1 %copy-start.4 = (f32[1,128,2]{1,2,0:T(2,128)S(1)}, f32[1,128,2]{1,2,0:T(2,128)}, u32[]{:S(2)}) copy-start(f32[1,128,2]{1,2,0:T(2,128)} %param.11) | copy-start | bytes 3076
  403.9 30.7 %all-to-all-start.3 = ((bf16[16,20,512]{2,1,0:T(8,128)(2,1)}), bf16[16,20,512]{2,1,0:T(8,128)(2,1)S(1)}, u32[]{:S(2)}, u32[]{:S(2)}) async-start(bf16[16,20,512]{2,1,0:T(8,128)(2,1)} %squeeze.33), calls=%async_computation.3 | async-start | bytes 786432 | tf_op jit(solution)/shard_map/all_to_all | solution.py:86
  434.6 29.7 %all-to-all-start.4 = ((bf16[16,20,512]{2,1,0:T(8,128)(2,1)}), bf16[16,20,512]{2,1,0:T(8,128)(2,1)S(1)}, u32[]{:S(2)}, u32[]{:S(2)}) async-start(bf16[16,20,512]{2,1,0:T(8,128)(2,1)} %squeeze.34), calls=%async_computation.4 | async-start | bytes 786432 | tf_op jit(solution)/shard_map/all_to_all | solution.py:87
  466.6 8.1 %collective-permute-start = (bf16[128,512]{1,0:T(8,128)(2,1)S(1)}, bf16[128,512]{1,0:T(8,128)(2,1)S(1)}, u32[]{:S(2)}, u32[]{:S(2)}) collective-permute-start(bf16[128,512]{1,0:T(8,128)(2,1)S(1)} %multiply_reduce_fusion), channel_id=1, source_target_pairs={{0,128},{128,256},{256,384},{384,0},{1,129},{129,257},{257,385},{3... | collective-permute-start | bytes 393224 | tf_op jit(solution)/shard_map/ppermute | solution.py:10
Sparse Core Ops, SparseCore 0:
  9.5 34.7 all-gather.2
